TPU v7x, 32 devices: a whole 2x2x4 slice. The times are simulated.
32 devices in a mesh: uv: 8 (over z, y), rep: 4 (over x, core).
Axes of the slice: x: 2, y: 2, z: 4, core: 2. Of those that a mesh axis runs over, the one named last changes fastest.
Arguments:
- visibilities: float32 [2, 32, 8, 16, 12], P(None, ('uv', 'rep')), may hold values from -6 to 6
- tile_counts: int32 [32, 8, 16], P(('uv', 'rep')), may hold values from 2 to 12, as said below
- w_plane: int32 [32, 8, 16, 12], P(('uv', 'rep')), may hold values from 0 to 63
- u_offset: int32 [32, 8, 16, 12], P(('uv', 'rep')), may hold values from 0 to 120
- v_offset: int32 [32, 8, 16, 12], P(('uv', 'rep')), may hold values from 0 to 120
- kernels: float32 [64, 128], replicated, may hold values from -2.5 to 2.5
Outputs:
- spectrum: float32 [2048, 2, 1024], P(('uv', 'rep'))
Inputs may be any that keep to these rules, and one draw needn't show every extreme that they name: `tile_counts`: every source device's list for tile 16//2 of destination column 4 holds 12 visibilities; tiles near the grid's centre are fuller than others.
All inputs are finite; a program needn't handle non-finite values.
Results may differ from a plain program's by a relative error of at most 0.0029.
Values may be sent and summed in bfloat16 or wider, within the bound.
No kernel may reach another device: no remote copies, remote signals or barrier semaphores. Data moves between devices by JAX's collectives and lax.ppermute only.
A program may use at most 192 MiB of HBM per device.

v0:
```python
import math
import jax
import jax.numpy as jnp
from jax import lax
from jax.sharding import PartitionSpec as P

TILE = 128
SUPPORT = 8


def weigh(vis_re, vis_im, planes, kernels):
    nplanes = kernels.shape[0]
    width = kernels.shape[1]
    half = width // 2
    onehot = (
        planes[..., None] == lax.broadcasted_iota(jnp.int32, planes.shape + (nplanes,), planes.ndim)
    ).astype(jnp.float32)
    kern = jnp.dot(
        onehot.reshape(-1, nplanes),
        kernels,
        precision=lax.Precision.HIGHEST,
        preferred_element_type=jnp.float32,
    )
    kern = kern.reshape(planes.shape + (width,))
    kern_re = kern[..., :half]
    kern_im = kern[..., half:]
    part_re = vis_re[..., None] * kern_re - vis_im[..., None] * kern_im
    part_im = vis_re[..., None] * kern_im + vis_im[..., None] * kern_re
    return jnp.concatenate([part_re, part_im], axis=-1).astype(jnp.bfloat16)


def grid_tiles(weighted, row_start, col_start):
    senders = weighted.shape[0]
    ntiles = weighted.shape[1]
    slots = weighted.shape[2]
    count = senders * slots
    per_tile = jnp.moveaxis(weighted, 1, 0).reshape(ntiles, count, 2, SUPPORT, SUPPORT)
    rows_all = jnp.moveaxis(row_start, 1, 0).reshape(ntiles, count)
    cols_all = jnp.moveaxis(col_start, 1, 0).reshape(ntiles, count)
    lanes = lax.broadcasted_iota(jnp.int32, (1, SUPPORT, TILE), 2)
    taps = lax.broadcasted_iota(jnp.int32, (1, SUPPORT, TILE), 1)
    cells = lax.broadcasted_iota(jnp.int32, (TILE, 1, SUPPORT), 0)
    taps_row = lax.broadcasted_iota(jnp.int32, (TILE, 1, SUPPORT), 2)

    def one_tile(operands):
        values, row_first, col_first = operands
        place = (lanes == col_first[:, None, None] + taps).astype(jnp.bfloat16)
        spread = jnp.einsum("ncij,njb->nicb", values, place)
        spread = spread.reshape(count * SUPPORT, 2 * TILE)
        pick = (cells == row_first[None, :, None] + taps_row).astype(jnp.bfloat16)
        pick = pick.reshape(TILE, count * SUPPORT)
        summed = jnp.dot(pick, spread, preferred_element_type=jnp.float32)
        return summed.reshape(TILE, 2, TILE)

    return lax.map(one_tile, (per_tile, rows_all, cols_all))


def make_table(first, second, length):
    index_a = lax.broadcasted_iota(jnp.int32, (first, second), 0)
    index_b = lax.broadcasted_iota(jnp.int32, (first, second), 1)
    angle = 2.0 * math.pi / length * (index_a * index_b % length).astype(jnp.float32)
    return (jnp.cos(angle), jnp.sin(angle))


def transform(pencil):
    nrows = pencil.shape[0]
    groups = lax.axis_size("uv")
    total = pencil.shape[2]
    width = total // groups
    highest = lax.Precision.HIGHEST
    cos_a, sin_a = make_table(groups, groups, groups)
    cos_t, sin_t = make_table(groups, width, total)
    cos_b, sin_b = make_table(width, width, width)
    field = pencil.reshape(nrows, 2, groups, width)
    real_in = field[:, 0]
    imag_in = field[:, 1]
    first_re = jnp.einsum("rpj,pk->rkj", real_in, cos_a, precision=highest) + jnp.einsum(
        "rpj,pk->rkj", imag_in, sin_a, precision=highest
    )
    first_im = jnp.einsum("rpj,pk->rkj", imag_in, cos_a, precision=highest) - jnp.einsum(
        "rpj,pk->rkj", real_in, sin_a, precision=highest
    )
    turned_re = first_re * cos_t + first_im * sin_t
    turned_im = first_im * cos_t - first_re * sin_t
    final_re = jnp.einsum("rkj,jm->rmk", turned_re, cos_b, precision=highest) + jnp.einsum(
        "rkj,jm->rmk", turned_im, sin_b, precision=highest
    )
    final_im = jnp.einsum("rkj,jm->rmk", turned_im, cos_b, precision=highest) - jnp.einsum(
        "rkj,jm->rmk", turned_re, sin_b, precision=highest
    )
    scale = 1.0 / math.sqrt(total)
    return (
        jnp.stack([final_re.reshape(nrows, total), final_im.reshape(nrows, total)], axis=1) * scale
    )


def shards(visibilities, tile_counts, w_plane, u_offset, v_offset, kernels):
    dests = visibilities.shape[2]
    ntiles = visibilities.shape[3]
    slots = visibilities.shape[4]
    nuv = lax.axis_size("uv")
    nrep = lax.axis_size("rep")
    per_device = ntiles * TILE // (nuv * nrep)
    live = (
        lax.broadcasted_iota(jnp.int32, (dests, ntiles, slots), 2) < tile_counts[0][:, :, None]
    ).astype(jnp.float32)
    vis_re = visibilities[0, 0] * live
    vis_im = visibilities[1, 0] * live
    weighted = weigh(vis_re, vis_im, w_plane[0], kernels)
    slab = grid_tiles(
        lax.all_to_all(weighted, "uv", split_axis=0, concat_axis=0, tiled=True),
        lax.all_to_all(u_offset[0], "uv", split_axis=0, concat_axis=0, tiled=True),
        lax.all_to_all(v_offset[0], "uv", split_axis=0, concat_axis=0, tiled=True),
    )
    blocks = slab.reshape(nuv, nrep, per_device, 2, TILE)
    moved_rows = lax.all_to_all(blocks, "uv", split_axis=0, concat_axis=4, tiled=True)
    pencil = lax.psum_scatter(moved_rows, "rep", scatter_dimension=1, tiled=True)
    pencil = pencil.reshape(per_device, 2, nuv * TILE)
    return transform(pencil)


def solution(mesh):
    placed = (
        P(None, ("uv", "rep"), None, None, None),
        P(("uv", "rep"), None, None),
        P(("uv", "rep"), None, None, None),
        P(("uv", "rep"), None, None, None),
        P(("uv", "rep"), None, None, None),
        P(),
    )
    return jax.shard_map(
        shards, mesh=mesh, in_specs=placed, out_specs=P(("uv", "rep"), None, None), check_vma=False
    )
```

profile of v0, /device:TPU:0, one launch (start us, length us, event | category | flops | bytes accessed | tf_op | source)
XLA Modules:
  0.0 184.7 jit_solution(3883717939173195149)
XLA Ops:
  8.1 7.3 %all-to-all-start = ((s32[8,1,192]{2,1,0:T(1,128)}), s32[8,1,192]{2,1,0:T(1,128)S(1)}, u32[]{:S(2)}, u32[]{:S(2)}) async-start(s32[8,1,192]{2,1,0:T(1,128)} %reshape.171), calls=%async_computation | async-start | bytes 16384 | tf_op jit(solution)/shard_map/all_to_all | solution.py:112
  15.3 0.8 bitcast_select_fusion.1
  19.3 2.6 %all-to-all-done = s32[8,1,192]{2,1,0:T(1,128)S(1)} async-done(((s32[8,1,192]{2,1,0:T(1,128)}), s32[8,1,192]{2,1,0:T(1,128)S(1)}, u32[]{:S(2)}, u32[]{:S(2)}) %all-to-all-start) | async-done | bytes 6176 | tf_op jit(solution)/shard_map/all_to_all | solution.py:112
  21.8 3.4 %all-to-all-start.1 = ((s32[8,1,192]{2,1,0:T(1,128)}), s32[8,1,192]{2,1,0:T(1,128)S(1)}, u32[]{:S(2)}, u32[]{:S(2)}) async-start(s32[8,1,192]{2,1,0:T(1,128)} %reshape.173), calls=%async_computation.1 | async-start | bytes 16384 | tf_op jit(solution)/shard_map/all_to_all | solution.py:113
  25.3 1.0 pad_maximum_fusion
  26.2 5.5 %all-to-all-done.1 = s32[8,1,192]{2,1,0:T(1,128)S(1)} async-done(((s32[8,1,192]{2,1,0:T(1,128)}), s32[8,1,192]{2,1,0:T(1,128)S(1)}, u32[]{:S(2)}, u32[]{:S(2)}) %all-to-all-start.1) | async-done | bytes 6176 | tf_op jit(solution)/shard_map/all_to_all | solution.py:113
  31.8 3.5 %all-to-all-start.2 = ((bf16[8,16,12,128]{3,1,2,0:T(8,128)(2,1)}), bf16[8,16,12,128]{3,1,2,0:T(8,128)(2,1)S(1)}, u32[]{:S(2)}, u32[]{:S(2)}) async-start(bf16[8,16,12,128]{3,1,2,0:T(8,128)(2,1)} %pad_maximum_fusion), calls=%async_computation.2 | async-start | bytes 786432 | tf_op jit(solution)/shard_map/all_to_all | solution.py:111
  37.6 7.5 %all-to-all-done.2 = bf16[8,16,12,128]{3,1,2,0:T(8,128)(2,1)S(1)} async-done(((bf16[8,16,12,128]{3,1,2,0:T(8,128)(2,1)}), bf16[8,16,12,128]{3,1,2,0:T(8,128)(2,1)S(1)}, u32[]{:S(2)}, u32[]{:S(2)}) %all-to-all-start.2) | async-done | bytes 393248 | tf_op jit(solution)/shard_map/all_to_all | solution.py:111
  45.3 8.5 %reshape.170 = bf16[16,96,2,8,8]{4,3,2,1,0:T(8,128)(2,1)} reshape(bf16[16,8,12,128]{3,2,1,0:T(8,128)(2,1)S(1)} %copy.99) | data formatting | bytes 786432
  53.7 31.8 %while.13 = (s32[]{:T(128)}, f32[16,128,2,128]{3,1,0,2:T(8,128)S(1)}, s32[16,96]{1,0:T(8,128)S(1)}, s32[16,96]{1,0:T(8,128)S(1)}, bf16[16,96,2,8,8]{4,3,2,1,0:T(8,128)(2,1)}, /*index=5*/s32[]{:T(128)}) while((s32[]{:T(128)}, f32[16,128,2,128]{3,1,0,2:T(8,128)S(1)}, s32[16,96]{1,0:T(8,128)S(1)}, s32[16,96]{1,0:T(8,128)S(1)}, ...), condition=%wide.region_1.2_spmd.clone.clone, body=%wide.region_0.1_spmd.clone.clone.sunk | while | flops 53773056 | bytes 2113357 | solution.py:55
  53.8 1.3 convolution_bitcast_fusion.3
  55.7 1.3 convolution_bitcast_fusion.3
  57.7 1.3 convolution_bitcast_fusion.3
  59.7 1.3 convolution_bitcast_fusion.3
  61.7 1.3 convolution_bitcast_fusion.3
  63.7 1.3 convolution_bitcast_fusion.3
  65.7 1.3 convolution_bitcast_fusion.3
  67.7 1.3 convolution_bitcast_fusion.3
  69.6 1.3 convolution_bitcast_fusion.3
  71.6 1.3 convolution_bitcast_fusion.3
  73.6 1.3 convolution_bitcast_fusion.3
  75.6 1.3 convolution_bitcast_fusion.3
  77.6 1.3 convolution_bitcast_fusion.3
  79.6 1.3 convolution_bitcast_fusion.3
  81.6 1.3 convolution_bitcast_fusion.3
  83.6 1.3 convolution_bitcast_fusion.3
  85.8 50.9 %all_to_all.33 = f32[8,4,64,2,128]{4,2,1,3,0:T(8,128)S(1)} all-to-all(f32[8,4,64,2,128]{4,2,1,3,0:T(8,128)S(1)} %copy.83), channel_id=1, replica_groups=mesh['uv'=8,'rep'=4] {'uv'}, dimensions={0} | all-to-all | bytes 4194304 | tf_op jit(solution)/shard_map/all_to_all | solution.py:116
  136.7 1.2 copy.84
  137.9 2.0 %copy.85 = f32[1,4,64,2,1024]{4,2,3,0,1:T(8,128)} copy(f32[1,4,64,2,1024]{4,0,3,2,1:T(1,128)S(1)} %bitcast.143) | data formatting | bytes 4194304 | tf_op jit(solution)/shard_map/all_to_all | solution.py:116
  139.9 30.4 %reduce-scatter.2.cloned.1.call-done = f32[1,1,64,2,1024]{4,2,3,0,1:T(8,128)} async-done(((f32[1,4,64,2,1024]{4,2,3,0,1:T(8,128)}), f32[1,1,64,2,1024]{4,2,3,0,1:T(8,128)}) %reduce-scatter.2.cloned.1.call-update) | async-done | bytes 524304 | tf_op jit(solution)/shard_map/reduce_scatter | solution.py:117
  170.4 1.1 copy.104
  176.7 1.2 copy.94
  (123 shorter events, 22.6 us)
Async XLA Ops:
  6.5 10.5 %copy-start = (f32[64,128]{1,0:T(8,128)S(1)}, f32[64,128]{1,0:T(8,128)}, u32[]{:S(2)}) copy-start(f32[64,128]{1,0:T(8,128)} %param.13) | copy-start | bytes 98308
  6.5 12.0 %copy-start.1 = (s32[1,8,16,12]{2,1,3,0:T(8,128)S(1)}, s32[1,8,16,12]{2,1,3,0:T(8,128)}, u32[]{:S(2)}) copy-start(s32[1,8,16,12]{2,1,3,0:T(8,128)} %param.12) | copy-start | bytes 18436
  8.1 13.8 %all-to-all-start = ((s32[8,1,192]{2,1,0:T(1,128)}), s32[8,1,192]{2,1,0:T(1,128)S(1)}, u32[]{:S(2)}, u32[]{:S(2)}) async-start(s32[8,1,192]{2,1,0:T(1,128)} %reshape.171), calls=%async_computation | async-start | bytes 16384 | tf_op jit(solution)/shard_map/all_to_all | solution.py:112
  21.8 9.9 %all-to-all-start.1 = ((s32[8,1,192]{2,1,0:T(1,128)}), s32[8,1,192]{2,1,0:T(1,128)S(1)}, u32[]{:S(2)}, u32[]{:S(2)}) async-start(s32[8,1,192]{2,1,0:T(1,128)} %reshape.173), calls=%async_computation.1 | async-start | bytes 16384 | tf_op jit(solution)/shard_map/all_to_all | solution.py:113
  31.8 13.4 %all-to-all-start.2 = ((bf16[8,16,12,128]{3,1,2,0:T(8,128)(2,1)}), bf16[8,16,12,128]{3,1,2,0:T(8,128)(2,1)S(1)}, u32[]{:S(2)}, u32[]{:S(2)}) async-start(bf16[8,16,12,128]{3,1,2,0:T(8,128)(2,1)} %pad_maximum_fusion), calls=%async_computation.2 | async-start | bytes 786432 | tf_op jit(solution)/shard_map/all_to_all | solution.py:111
  35.2 135.1 %reduce-scatter.2.cloned.1.call-start = ((), (), s32[]{:S(2)}) async-start(), calls=%async_computation.5 | async-start | bytes 2621440 | tf_op jit(solution)/shard_map/reduce_scatter | solution.py:117
Sparse Core Ops, SparseCore 0:
  140.0 30.3 reduce-scatter.1
where the time goes:
time: 186 us; the launch traced here: 185 us
  blocking collectives  50.9 us (27%)
  waiting for transfers between devices  46.1 us (25%)
  matrix products  30.6 us (16%)
  local copies, waits for them, and re-layouts  23.5 us (13%)
  starting transfers between devices  14.2 us (8%)
  between operations  13.7 us (7%)
  other arithmetic  5.16 us (3%)
    all_to_all x1, blocking collectives, shards(): lax.all_to_all(blocks, 'uv', split_axis=0, concat_axis=4, tiled=True)  50.9 us
    reduce_scatter x1, waiting for transfers between devices, shards(): lax.psum_scatter(moved_rows, 'rep', scatter_dimension=1, tiled=True)  30.4 us
    dot_general x16, matrix products, one_tile(): spread = jnp.einsum('ncij,njb->nicb', values, place)  20.9 us
    unnamed x13, local copies, waits for them, and re-layouts  12.1 us
    all_to_all x1, waiting for transfers between devices, shards(): lax.all_to_all(weighted, 'uv', split_axis=0, concat_axis=0, tiled=True)  7.5 us
    all_to_all x1, starting transfers between devices, shards(): lax.all_to_all(u_offset[0], 'uv', split_axis=0, concat_axis=0, tiled=True)  7.28 us
    all_to_all x1, waiting for transfers between devices, shards(): lax.all_to_all(v_offset[0], 'uv', split_axis=0, concat_axis=0, tiled=True)  5.54 us
    dot_general x16, matrix products, one_tile(): summed = jnp.dot(pick, spread, preferred_element_type=jnp.float32)  4.67 us
  transfers between devices with their start and end apart: 4, of which 4 were waited for; matrix products, arithmetic and copies ran while one was open for 4% of the time, Pallas kernels for 0%

commit v1 on v0

--- a/solution.py
+++ b/solution.py
@@ -6,6 +6,28 @@
 
 TILE = 128
 SUPPORT = 8
+
+
+def split_up(x, dim, count):
+    before, after = (x.shape[:dim], x.shape[dim + 1 :])
+    return jnp.moveaxis(x.reshape(*before, count, -1, *after), dim, 0)
+
+
+def joined_along(tiles, dim):
+    tiles = jnp.moveaxis(tiles, 0, dim)
+    shape = tiles.shape
+    return tiles.reshape(*shape[:dim], shape[dim] * shape[dim + 1], *shape[dim + 2 :])
+
+
+def sent_to_each(x, axis, split_dim, concat_dim):
+    size, mine = (lax.axis_size(axis), lax.axis_index(axis))
+    parts = split_up(x, split_dim, size)
+    outs = [parts[mine]]
+    for step in range(1, size):
+        sent = parts[(mine + step) % size]
+        outs.append(lax.ppermute(sent, axis, [(i, (i + step) % size) for i in range(size)]))
+    parts = jnp.stack(outs)[(mine - jnp.arange(size)) % size]
+    return joined_along(parts, concat_dim)
 
 
 def weigh(vis_re, vis_im, planes, kernels):
@@ -109,7 +131,7 @@
     weighted = weigh(vis_re, vis_im, w_plane[0], kernels)
     slab = grid_tiles(
         lax.all_to_all(weighted, "uv", split_axis=0, concat_axis=0, tiled=True),
-        lax.all_to_all(u_offset[0], "uv", split_axis=0, concat_axis=0, tiled=True),
+        sent_to_each(u_offset[0], "uv", 0, 0),
         lax.all_to_all(v_offset[0], "uv", split_axis=0, concat_axis=0, tiled=True),
     )
     blocks = slab.reshape(nuv, nrep, per_device, 2, TILE)

time: 186 us -> 184 us (0.989)
  waiting for transfers between devices: 46.1 us -> 34.8 us
  starting transfers between devices: 14.2 us -> 25.2 us
    ppermute x0 -> x7, starting transfers between devices: none -> 14.2 us  [sent_to_each(): lax.ppermute(sent, axis, [(i, (i + step) % size) for i in range(size)])]
    all_to_all x1, waiting for transfers between devices: 7.5 us -> 0.01 us  [shards(): lax.all_to_all(weighted, 'uv', split_axis=0, concat_axis=0, tiled=True)]
    all_to_all x1 -> x0, starting transfers between devices: 7.28 us -> none  [shards(): lax.all_to_all(u_offset[0], 'uv', split_axis=0, concat_axis=0, tiled=True)]
    all_to_all x1, starting transfers between devices: 3.42 us -> 7.28 us  [shards(): lax.all_to_all(v_offset[0], 'uv', split_axis=0, concat_axis=0, tiled=True)]
    all_to_all x1, waiting for transfers between devices: 5.54 us -> 2.33 us  [shards(): lax.all_to_all(v_offset[0], 'uv', split_axis=0, concat_axis=0, tiled=True)]
    all_to_all x1 -> x0, waiting for transfers between devices: 2.59 us -> none  [shards(): lax.all_to_all(u_offset[0], 'uv', split_axis=0, concat_axis=0, tiled=True)]
    ppermute x0 -> x7, waiting for transfers between devices: none -> 1.92 us  [sent_to_each(): lax.ppermute(sent, axis, [(i, (i + step) % size) for i in range(size)])]
    unnamed x13 -> x10, local copies, waits for them, and re-layouts: 12.1 us -> 11.4 us
  transfers between devices with their start and end apart: 4 -> 10, of which waited for: 4 -> 3; matrix products, arithmetic and copies ran while one was open for 4% -> 3% of each run, Pallas kernels for 0% -> 0%
where the time goes in v1:
time: 184 us; the launch traced here: 182 us
  blocking collectives  49.6 us (27%)
  waiting for transfers between devices  34.8 us (19%)
  matrix products  30.6 us (17%)
  starting transfers between devices  25.2 us (14%)
  local copies, waits for them, and re-layouts  23.5 us (13%)
  between operations  13.8 us (8%)
  other arithmetic  4.33 us (2%)
    all_to_all x1, blocking collectives, shards(): lax.all_to_all(blocks, 'uv', split_axis=0, concat_axis=4, tiled=True)  49.6 us
    reduce_scatter x1, waiting for transfers between devices, shards(): lax.psum_scatter(moved_rows, 'rep', scatter_dimension=1, tiled=True)  30.5 us
    dot_general x16, matrix products, one_tile(): spread = jnp.einsum('ncij,njb->nicb', values, place)  20.9 us
    ppermute x7, starting transfers between devices, sent_to_each(): lax.ppermute(sent, axis, [(i, (i + step) % size) for i in range(size)])  14.2 us
    unnamed x10, local copies, waits for them, and re-layouts  11.4 us
    all_to_all x1, starting transfers between devices, shards(): lax.all_to_all(v_offset[0], 'uv', split_axis=0, concat_axis=0, tiled=True)  7.28 us
    dot_general x16, matrix products, one_tile(): summed = jnp.dot(pick, spread, preferred_element_type=jnp.float32)  4.67 us
  transfers between devices with their start and end apart: 10, of which 3 were waited for; matrix products, arithmetic and copies ran while one was open for 3% of the time, Pallas kernels for 0%

profile of v1, /device:TPU:0, one launch (start us, length us, event | category | flops | bytes accessed | tf_op | source)
XLA Modules:
  0.0 182.4 jit_solution(13228872202872873279)
XLA Ops:
  8.1 7.3 %all-to-all-start = ((s32[8,1,192]{2,1,0:T(1,128)}), s32[8,1,192]{2,1,0:T(1,128)S(1)}, u32[]{:S(2)}, u32[]{:S(2)}) async-start(s32[8,1,192]{2,1,0:T(1,128)} %reshape.249), calls=%async_computation | async-start | bytes 16384 | tf_op jit(solution)/shard_map/all_to_all | solution.py:135
  19.5 2.3 %all-to-all-done = s32[8,1,192]{2,1,0:T(1,128)S(1)} async-done(((s32[8,1,192]{2,1,0:T(1,128)}), s32[8,1,192]{2,1,0:T(1,128)S(1)}, u32[]{:S(2)}, u32[]{:S(2)}) %all-to-all-start) | async-done | bytes 6176 | tf_op jit(solution)/shard_map/all_to_all | solution.py:135
  21.9 3.7 %all-to-all-start.1 = ((bf16[8,16,12,128]{3,1,2,0:T(8,128)(2,1)}), bf16[8,16,12,128]{3,1,2,0:T(8,128)(2,1)S(1)}, u32[]{:S(2)}, u32[]{:S(2)}) async-start(bf16[8,16,12,128]{3,1,2,0:T(8,128)(2,1)} %pad_maximum_fusion), calls=%async_computation.1 | async-start | bytes 786432 | tf_op jit(solution)/shard_map/all_to_all | solution.py:133
  25.7 3.7 %collective-permute-start.4 = (s32[1,16,12]{1,0,2:T(1,128)S(1)}, s32[1,16,12]{1,0,2:T(1,128)S(1)}, u32[]{:S(2)}, u32[]{:S(2)}) collective-permute-start(s32[1,16,12]{1,0,2:T(1,128)S(1)} %get-tuple-element.152), channel_id=1, source_target_pairs={{0,20},{4,24},{8,28},{12,0},{16,4},{20,8},{24,12},{28,16},{1,21},{... | collective-permute-start | bytes 2312 | tf_op jit(solution)/shard_map/ppermute | solution.py:28
  29.5 1.5 collective-permute-start.5
  31.5 1.5 collective-permute-start
  33.5 3.8 %collective-permute-start.2 = (s32[1,16,12]{1,0,2:T(1,128)S(1)}, s32[1,16,12]{1,0,2:T(1,128)S(1)}, u32[]{:S(2)}, u32[]{:S(2)}) collective-permute-start(s32[1,16,12]{1,0,2:T(1,128)S(1)} %get-tuple-element.154), channel_id=1, source_target_pairs={{0,12},{4,16},{8,20},{12,24},{16,28},{20,0},{24,4},{28,8},{1,13},{... | collective-permute-start | bytes 2312 | tf_op jit(solution)/shard_map/ppermute | solution.py:28
  37.3 2.6 %collective-permute-start.3 = (s32[1,16,12]{1,0,2:T(1,128)S(1)}, s32[1,16,12]{1,0,2:T(1,128)S(1)}, u32[]{:S(2)}, u32[]{:S(2)}) collective-permute-start(s32[1,16,12]{1,0,2:T(1,128)S(1)} %get-tuple-element.153), channel_id=1, source_target_pairs={{0,16},{4,20},{8,24},{12,28},{16,0},{20,4},{24,8},{28,12},{1,17},{... | collective-permute-start | bytes 2312 | tf_op jit(solution)/shard_map/ppermute | solution.py:28
  40.0 1.9 %collective-permute-done.3 = s32[1,16,12]{1,0,2:T(1,128)S(1)} collective-permute-done((s32[1,16,12]{1,0,2:T(1,128)S(1)}, s32[1,16,12]{1,0,2:T(1,128)S(1)}, u32[]{:S(2)}, u32[]{:S(2)}) %collective-permute-start.3) | collective-permute-done | bytes 800 | tf_op jit(solution)/shard_map/ppermute | solution.py:28
  44.1 8.5 %reshape.248 = bf16[16,96,2,8,8]{4,3,2,1,0:T(8,128)(2,1)} reshape(bf16[16,8,12,128]{3,2,1,0:T(8,128)(2,1)S(1)} %copy.103) | data formatting | bytes 786432
  52.6 31.8 %while.13 = (s32[]{:T(128)}, f32[16,128,2,128]{3,1,0,2:T(8,128)S(1)}, s32[16,96]{1,0:T(8,128)S(1)}, s32[16,96]{1,0:T(8,128)S(1)}, bf16[16,96,2,8,8]{4,3,2,1,0:T(8,128)(2,1)}, /*index=5*/s32[]{:T(128)}) while((s32[]{:T(128)}, f32[16,128,2,128]{3,1,0,2:T(8,128)S(1)}, s32[16,96]{1,0:T(8,128)S(1)}, s32[16,96]{1,0:T(8,128)S(1)}, ...), condition=%wide.region_1.2_spmd.clone.clone, body=%wide.region_0.1_spmd.clone.clone.sunk | while | flops 53773056 | bytes 2113357 | solution.py:77
  52.6 1.3 convolution_bitcast_fusion.3
  54.6 1.3 convolution_bitcast_fusion.3
  56.6 1.3 convolution_bitcast_fusion.3
  58.6 1.3 convolution_bitcast_fusion.3
  60.6 1.3 convolution_bitcast_fusion.3
  62.6 1.3 convolution_bitcast_fusion.3
  64.6 1.3 convolution_bitcast_fusion.3
  66.5 1.3 convolution_bitcast_fusion.3
  68.5 1.3 convolution_bitcast_fusion.3
  70.5 1.3 convolution_bitcast_fusion.3
  72.5 1.3 convolution_bitcast_fusion.3
  74.5 1.3 convolution_bitcast_fusion.3
  76.5 1.3 convolution_bitcast_fusion.3
  78.5 1.3 convolution_bitcast_fusion.3
  80.5 1.3 convolution_bitcast_fusion.3
  82.4 1.3 convolution_bitcast_fusion.3
  84.7 49.6 %all_to_all.28 = f32[8,4,64,2,128]{4,2,1,3,0:T(8,128)S(1)} all-to-all(f32[8,4,64,2,128]{4,2,1,3,0:T(8,128)S(1)} %copy.88), channel_id=1, replica_groups=mesh['uv'=8,'rep'=4] {'uv'}, dimensions={0} | all-to-all | bytes 4194304 | tf_op jit(solution)/shard_map/all_to_all | solution.py:138
  134.3 1.2 copy.89
  135.5 2.0 %copy.90 = f32[1,4,64,2,1024]{4,2,3,0,1:T(8,128)} copy(f32[1,4,64,2,1024]{4,0,3,2,1:T(1,128)S(1)} %bitcast.156) | data formatting | bytes 4194304 | tf_op jit(solution)/shard_map/all_to_all | solution.py:138
  137.6 30.5 %reduce-scatter.2.cloned.1.call-done = f32[1,1,64,2,1024]{4,2,3,0,1:T(8,128)} async-done(((f32[1,4,64,2,1024]{4,2,3,0,1:T(8,128)}), f32[1,1,64,2,1024]{4,2,3,0,1:T(8,128)}) %reduce-scatter.2.cloned.1.call-update) | async-done | bytes 524304 | tf_op jit(solution)/shard_map/reduce_scatter | solution.py:139
  174.4 1.2 copy.99
  (136 shorter events, 25.8 us)
Async XLA Ops:
  6.5 10.5 %copy-start = (f32[64,128]{1,0:T(8,128)S(1)}, f32[64,128]{1,0:T(8,128)}, u32[]{:S(2)}) copy-start(f32[64,128]{1,0:T(8,128)} %param.13) | copy-start | bytes 98308
  8.1 13.8 %all-to-all-start = ((s32[8,1,192]{2,1,0:T(1,128)}), s32[8,1,192]{2,1,0:T(1,128)S(1)}, u32[]{:S(2)}, u32[]{:S(2)}) async-start(s32[8,1,192]{2,1,0:T(1,128)} %reshape.249), calls=%async_computation | async-start | bytes 16384 | tf_op jit(solution)/shard_map/all_to_all | solution.py:135
  17.9 7.8 %copy-start.1 = (s32[1,8,16,12]{2,1,3,0:T(8,128)S(1)}, s32[1,8,16,12]{2,1,3,0:T(8,128)}, u32[]{:S(2)}) copy-start(s32[1,8,16,12]{2,1,3,0:T(8,128)} %param.11) | copy-start | bytes 18436
  21.9 22.1 %all-to-all-start.1 = ((bf16[8,16,12,128]{3,1,2,0:T(8,128)(2,1)}), bf16[8,16,12,128]{3,1,2,0:T(8,128)(2,1)S(1)}, u32[]{:S(2)}, u32[]{:S(2)}) async-start(bf16[8,16,12,128]{3,1,2,0:T(8,128)(2,1)} %pad_maximum_fusion), calls=%async_computation.1 | async-start | bytes 786432 | tf_op jit(solution)/shard_map/all_to_all | solution.py:133
  25.5 142.6 %reduce-scatter.2.cloned.1.call-start = ((), (), s32[]{:S(2)}) async-start(), calls=%async_computation.4 | async-start | bytes 2621440 | tf_op jit(solution)/shard_map/reduce_scatter | solution.py:139
  25.7 7.8 %collective-permute-start.4 = (s32[1,16,12]{1,0,2:T(1,128)S(1)}, s32[1,16,12]{1,0,2:T(1,128)S(1)}, u32[]{:S(2)}, u32[]{:S(2)}) collective-permute-start(s32[1,16,12]{1,0,2:T(1,128)S(1)} %get-tuple-element.152), channel_id=1, source_target_pairs={{0,20},{4,24},{8,28},{12,0},{16,4},{20,8},{24,12},{28,16},{1,21},{... | collective-permute-start | bytes 2312 | tf_op jit(solution)/shard_map/ppermute | solution.py:28
  29.5 7.9 %collective-permute-start.5 = (s32[1,16,12]{1,0,2:T(1,128)S(1)}, s32[1,16,12]{1,0,2:T(1,128)S(1)}, u32[]{:S(2)}, u32[]{:S(2)}) collective-permute-start(s32[1,16,12]{1,0,2:T(1,128)S(1)} %get-tuple-element.158), channel_id=1, source_target_pairs={{0,24},{4,28},{8,0},{12,4},{16,8},{20,12},{24,16},{28,20},{1,25},{... | collective-permute-start | bytes 2312 | tf_op jit(solution)/shard_map/ppermute | solution.py:28
  30.9 9.0 %collective-permute-start.6 = (s32[1,16,12]{1,0,2:T(1,128)S(1)}, s32[1,16,12]{1,0,2:T(1,128)S(1)}, u32[]{:S(2)}, u32[]{:S(2)}) collective-permute-start(s32[1,16,12]{1,0,2:T(1,128)S(1)} %get-tuple-element.151), channel_id=1, source_target_pairs={{0,28},{4,0},{8,4},{12,8},{16,12},{20,16},{24,20},{28,24},{1,29},{... | collective-permute-start | bytes 2312 | tf_op jit(solution)/shard_map/ppermute | solution.py:28
  31.5 8.5 %collective-permute-start = (s32[1,16,12]{1,0,2:T(1,128)S(1)}, s32[1,16,12]{1,0,2:T(1,128)S(1)}, u32[]{:S(2)}, u32[]{:S(2)}) collective-permute-start(s32[1,16,12]{1,0,2:T(1,128)S(1)} %get-tuple-element.156), channel_id=1, source_target_pairs={{0,4},{4,8},{8,12},{12,16},{16,20},{20,24},{24,28},{28,0},{1,5},{5... | collective-permute-start | bytes 2312 | tf_op jit(solution)/shard_map/ppermute | solution.py:28
  33.0 7.0 %collective-permute-start.1 = (s32[1,16,12]{1,0,2:T(1,128)S(1)}, s32[1,16,12]{1,0,2:T(1,128)S(1)}, u32[]{:S(2)}, u32[]{:S(2)}) collective-permute-start(s32[1,16,12]{1,0,2:T(1,128)S(1)} %get-tuple-element.155), channel_id=1, source_target_pairs={{0,8},{4,12},{8,16},{12,20},{16,24},{20,28},{24,0},{28,4},{1,9},{5... | collective-permute-start | bytes 2312 | tf_op jit(solution)/shard_map/ppermute | solution.py:28
  33.5 6.4 %collective-permute-start.2 = (s32[1,16,12]{1,0,2:T(1,128)S(1)}, s32[1,16,12]{1,0,2:T(1,128)S(1)}, u32[]{:S(2)}, u32[]{:S(2)}) collective-permute-start(s32[1,16,12]{1,0,2:T(1,128)S(1)} %get-tuple-element.154), channel_id=1, source_target_pairs={{0,12},{4,16},{8,20},{12,24},{16,28},{20,0},{24,4},{28,8},{1,13},{... | collective-permute-start | bytes 2312 | tf_op jit(solution)/shard_map/ppermute | solution.py:28
  37.3 4.5 %collective-permute-start.3 = (s32[1,16,12]{1,0,2:T(1,128)S(1)}, s32[1,16,12]{1,0,2:T(1,128)S(1)}, u32[]{:S(2)}, u32[]{:S(2)}) collective-permute-start(s32[1,16,12]{1,0,2:T(1,128)S(1)} %get-tuple-element.153), channel_id=1, source_target_pairs={{0,16},{4,20},{8,24},{12,28},{16,0},{20,4},{24,8},{28,12},{1,17},{... | collective-permute-start | bytes 2312 | tf_op jit(solution)/shard_map/ppermute | solution.py:28
Sparse Core Ops, SparseCore 0:
  137.6 30.4 reduce-scatter.1
